TPU v7x, 512 devices: a whole 4x4x16 slice. The times are simulated.
512 devices in a mesh: replica: 64 (over z, x), shard: 8 (over y, core).
Axes of the slice: x: 4, y: 4, z: 16, core: 2. Of those that a mesh axis runs over, the one named last changes fastest.
Arguments:
- grad_query: float32 [512, 512, 384], P(('replica', 'shard')), may hold values from -1.25 to 1.25
- grad_output: float32 [512, 384, 512], P(('replica', 'shard')), may hold values from -1.25 to 1.25
- grad_norm: float32 [512, 512], P(('replica', 'shard')), may hold values from -1.25 to 1.25
- grad_bias: float32 [512, 32, 6], P(('replica', 'shard')), may hold values from -0.3 to 0.3
- weight_query: float32 [512, 384], P('shard'), may hold values from -5.303301 to 5.303301
- weight_output: float32 [384, 512], P('shard'), may hold values from -6.1237244 to 6.1237244
- weight_norm: float32 [512], P('shard'), may hold values from 0 to 120
- weight_bias: float32 [32, 6], P('shard'), may hold values from -120 to 120
- first_query: float32 [512, 384], P('shard'), may hold values from -120 to 120
- first_output: float32 [384, 512], P('shard'), may hold values from -120 to 120
- first_norm: float32 [512], P('shard'), may hold values from -120 to 120
- first_bias: float32 [32, 6], P('shard'), may hold values from -120 to 120
- second_query: float32 [512, 384], P('shard'), may hold values from 0.05 to 2
- second_output: float32 [384, 512], P('shard'), may hold values from 0.05 to 2
- second_norm: float32 [512], P('shard'), may hold values from 0.05 to 2
- second_bias: float32 [32, 6], P('shard'), may hold values from 0.05 to 2
Outputs:
- updated_query: bfloat16 [512, 384], replicated
- updated_output: bfloat16 [384, 512], replicated
- updated_norm: bfloat16 [512], replicated
- updated_bias: bfloat16 [32, 6], replicated
- first_query_next: float32 [512, 384], P('shard')
- first_output_next: float32 [384, 512], P('shard')
- first_norm_next: float32 [512], P('shard')
- first_bias_next: float32 [32, 6], P('shard')
- second_query_next: float32 [512, 384], P('shard')
- second_output_next: float32 [384, 512], P('shard')
- second_norm_next: float32 [512], P('shard')
- second_bias_next: float32 [32, 6], P('shard')
- norm_table: float32 [2, 4], replicated
- trust_ratios: float32 [4], replicated
All inputs are finite; a program needn't handle non-finite values.
Results may differ from a plain program's by a relative error of at most 0.008.
Values may be sent and summed in bfloat16 or wider, within the bound.
No kernel may reach another device: no remote copies, remote signals or barrier semaphores. Data moves between devices by JAX's collectives and lax.ppermute only.
A program may use at most 64 MiB of HBM per device.

v0:
```python
import jax
import jax.numpy as jnp
from jax import lax
from jax.sharding import PartitionSpec as P


def step_math(summed, moment, second, weight, decay_rate):
    moment_next = 0.5 * moment + 0.5 * summed
    second_next = 0.5 * second + 0.5 * summed * summed
    update = moment_next / (jnp.sqrt(second_next) + 1e-06) + decay_rate * weight
    return (moment_next, second_next, update)


def on_device(
    grad_query,
    grad_output,
    grad_norm,
    grad_bias,
    weight_query,
    weight_output,
    weight_norm,
    weight_bias,
    first_query,
    first_output,
    first_norm,
    first_bias,
    second_query,
    second_output,
    second_norm,
    second_bias,
):
    weights = (weight_query, weight_output, weight_norm, weight_bias)
    moments = (first_query, first_output, first_norm, first_bias)
    seconds = (second_query, second_output, second_norm, second_bias)
    decay_rates = (0.01, 0.01, 0.0, 0.0)
    gradients = (grad_query[0], grad_output[0], grad_norm[0], grad_bias[0])
    totals = lax.psum(
        (gradients[0], gradients[1], gradients[2], gradients[3]), ("replica", "shard")
    )
    position = lax.axis_index("shard")
    summed_all = tuple(
        (
            lax.dynamic_slice_in_dim(entire, position * weight.shape[0], weight.shape[0], 0)
            for entire, weight in zip(totals, weights)
        )
    )
    results = [
        step_math(
            summed_all[member],
            moments[member],
            seconds[member],
            weights[member],
            decay_rates[member],
        )
        for member in range(4)
    ]
    weight_squares = [jnp.sum(weight * weight) for weight in weights]
    update_squares = [jnp.sum(result[2] * result[2]) for result in results]
    couples = [
        lax.psum((weight_squares[member], update_squares[member]), "shard") for member in range(4)
    ]
    weight_sizes = jnp.sqrt(jnp.stack([couple[0] for couple in couples]))
    update_sizes = jnp.sqrt(jnp.stack([couple[1] for couple in couples]))
    trust_ratios = weight_sizes / (update_sizes + 1e-06)
    shards = tuple(
        (
            (weights[member] - 0.01 * trust_ratios[member] * results[member][2]).astype(
                jnp.bfloat16
            )
            for member in range(4)
        )
    )
    gathered = (
        lax.all_gather(shards[0], "shard", axis=0, tiled=True),
        lax.all_gather(shards[1], "shard", axis=0, tiled=True),
        lax.all_gather(shards[2], "shard", axis=0, tiled=True),
        lax.all_gather(shards[3], "shard", axis=0, tiled=True),
    )
    norm_table = jnp.stack([weight_sizes, update_sizes])
    return (
        gathered[0],
        gathered[1],
        gathered[2],
        gathered[3],
        results[0][0],
        results[1][0],
        results[2][0],
        results[3][0],
        results[0][1],
        results[1][1],
        results[2][1],
        results[3][1],
        norm_table,
        trust_ratios,
    )


def solution(mesh):
    placed = (
        P(("replica", "shard"), None, None),
        P(("replica", "shard"), None, None),
        P(("replica", "shard"), None),
        P(("replica", "shard"), None, None),
        P("shard", None),
        P("shard", None),
        P("shard"),
        P("shard", None),
        P("shard", None),
        P("shard", None),
        P("shard"),
        P("shard", None),
        P("shard", None),
        P("shard", None),
        P("shard"),
        P("shard", None),
    )
    return jax.shard_map(
        on_device,
        mesh=mesh,
        in_specs=placed,
        out_specs=(
            P(),
            P(),
            P(),
            P(),
            P("shard", None),
            P("shard", None),
            P("shard"),
            P("shard", None),
            P("shard", None),
            P("shard", None),
            P("shard"),
            P("shard", None),
            P(),
            P(),
        ),
        check_vma=False,
    )
```

profile of v0, /device:TPU:1, one launch (start us, length us, event | category | flops | bytes accessed | tf_op | source)
XLA Modules:
  0.0 580.5 jit_solution(12802664677548248440)
XLA Ops:
  7.2 0.0 all-reduce.6.cloned.1.call-start
  7.2 0.0 copy-start.12
  7.2 0.0 copy-start.13
  7.2 0.0 copy-start.14
  7.3 0.0 copy-start.17
  7.3 0.0 copy-start.18
  7.3 0.0 copy-start.11
  7.3 0.0 copy-start.15
  7.3 0.0 copy-start.16
  7.3 0.0 copy-start.6
  7.3 0.0 copy-start.7
  7.3 0.6 all-reduce.6.cloned.1.call-update
  7.9 0.0 copy-start
  7.9 0.0 copy-done.12
  7.9 0.1 copy.32
  8.0 1.3 dynamic-slice
  9.9 0.0 copy-done.13
  10.0 111.8 %all-reduce.1 = (f32[32,6]{1,0:T(8,128)S(1)}, f32[512]{0:T(512)S(1)}) all-reduce(f32[32,6]{1,0:T(8,128)S(1)} %bitcast.30, f32[512]{0:T(512)S(1)} %bitcast.32), channel_id=1, replica_groups=mesh['replica'=64,'shard'=8] {'replica','shard'}, use_global_device_ids=true, to_apply=%region_17.0 | all-reduce | flops 704 | bytes 5632 | tf_op jit(solution)/shard_map/psum | solution.py:37
  121.8 0.0 copy-done.14
  121.8 0.0 copy-done.17
  121.8 0.0 copy-done.18
  121.8 1.2 multiply_reduce_fusion.6
  123.0 0.0 copy-done.11
  123.0 0.0 copy-done.15
  123.0 0.0 copy-done.16
  123.0 1.2 multiply_reduce_fusion.4
  124.2 366.8 %all-reduce.6.cloned.1.call-done = (f32[384,512]{1,0:T(8,128)}, f32[512,384]{1,0:T(8,128)}) async-done(((f32[384,512]{1,0:T(8,128)}, f32[512,384]{1,0:T(8,128)}), (f32[384,512]{1,0:T(8,128)}, f32[512,384]{1,0:T(8,128)})) %all-reduce.6.cloned.1.call-update) | async-done | bytes 1572880 | tf_op jit(solution)/shard_map/psum | solution.py:37
  490.9 0.0 copy-done.6
  490.9 0.0 copy-done.7
  490.9 0.0 copy-done
  491.0 0.0 copy-start.1
  491.0 0.0 copy-start.8
  491.0 0.0 copy-start.9
  491.0 1.7 multiply_reduce_fusion.1
  492.7 0.0 copy-start.2
  492.7 0.0 copy-start.3
  492.7 0.0 copy-done.1
  492.7 0.0 copy-done.8
  492.7 0.0 copy-done.9
  492.7 1.6 multiply_reduce_fusion
  494.4 0.0 copy-start.4
  494.4 0.0 copy-start.5
  494.4 14.6 %all-reduce.3 = (f32[]{:T(128)}, f32[]{:T(128)}, f32[]{:T(128)}, f32[]{:T(128)}, f32[]{:T(128)}, /*index=5*/f32[]{:T(128)}, f32[]{:T(128)}, f32[]{:T(128)}) all-reduce(f32[]{:T(128)} %get-tuple-element.70, f32[]{:T(128)} %get-tuple-element.75, f32[]{:T(128)} %get-tuple-element.45, ...), channel_id=1, replica_groups=mesh['replica'=64,'shard'=8] {'shard'}, use_global_device_ids=true, to_apply=%region_7.0 | all-reduce | flops 8 | bytes 64 | tf_op jit(solution)/shard_map/psum | solution.py:60
  508.9 5.1 fusion.5
  514.1 0.0 copy-start.10
  514.1 0.6 fusion.11
  514.7 0.0 copy-done.10
  515.3 0.0 copy-done.2
  515.3 0.0 copy-done.3
  515.3 0.1 subtract_convert_fusion.1
  515.4 14.0 %all_gather.12 = bf16[512,384]{1,0:T(8,128)(2,1)S(1)} all-gather(bf16[64,384]{1,0:T(8,128)(2,1)S(1)} %subtract_convert_fusion.1), channel_id=1, replica_groups=mesh['replica'=64,'shard'=8] {'shard'}, dimensions={0}, use_global_device_ids=true | all-gather | bytes 442368 | tf_op jit(solution)/shard_map/all_gather | solution.py:74
  530.0 0.0 copy-done.4
  530.0 0.0 copy-done.5
  530.0 0.1 subtract_convert_fusion
  530.1 13.0 %all_gather.13 = bf16[384,512]{1,0:T(8,128)(2,1)S(1)} all-gather(bf16[48,512]{1,0:T(8,128)(2,1)S(1)} %subtract_convert_fusion), channel_id=1, replica_groups=mesh['replica'=64,'shard'=8] {'shard'}, dimensions={0}, use_global_device_ids=true | all-gather | bytes 442368 | tf_op jit(solution)/shard_map/all_gather | solution.py:75
  543.7 0.2 dynamic-update-slice
  544.0 12.5 %all-reduce = bf16[512]{0:T(512)(128)(2,1)} all-reduce(bf16[512]{0:T(512)(128)(2,1)S(1)} %dynamic-update-slice), channel_id=1, replica_groups=mesh['replica'=64,'shard'=8] {'shard'}, use_global_device_ids=true, to_apply=%add | all-reduce | flops 512 | bytes 2048
  557.1 8.6 %all-gather = bf16[8,4,6]{2,1,0:T(4,128)(2,1)S(1)} all-gather(bf16[1,4,6]{2,1,0:T(4,128)(2,1)S(1)} %fusion.3), channel_id=1, replica_groups=mesh['replica'=64,'shard'=8] {'shard'}, dimensions={0}, use_global_device_ids=true | all-gather | bytes 432 | tf_op jit(solution)/shard_map/all_gather | solution.py:77
  565.7 0.7 copy.33
  566.4 5.1 maximum_sqrt_fusion.2
  571.5 0.6 pad_maximum_fusion
  572.1 0.7 copy.41
  572.9 0.7 copy.42
  (3 shorter events, 0.0 us)
Async XLA Ops:
  7.2 483.8 %all-reduce.6.cloned.1.call-start = ((), (), s32[]{:S(2)}) async-start(), calls=%async_computation | async-start | bytes 3145728 | tf_op jit(solution)/shard_map/psum | solution.py:37
  7.2 0.7 copy-start.12
  7.2 2.7 copy-start.13
  7.2 114.5 %copy-start.14 = (f32[64]{0:T(128)S(1)}, f32[64]{0:T(128)}, u32[]{:S(2)}) copy-start(f32[64]{0:T(128)} %param.22) | copy-start | bytes 772
  7.3 114.5 %copy-start.17 = (f32[64]{0:T(128)S(1)}, f32[64]{0:T(128)}, u32[]{:S(2)}) copy-start(f32[64]{0:T(128)} %param.30) | copy-start | bytes 772
  7.3 114.5 %copy-start.18 = (f32[64]{0:T(128)S(1)}, f32[64]{0:T(128)}, u32[]{:S(2)}) copy-start(f32[64]{0:T(128)} %param.26) | copy-start | bytes 772
  7.3 115.7 %copy-start.11 = (f32[4,6]{1,0:T(4,128)S(1)}, f32[4,6]{1,0:T(4,128)}, u32[]{:S(2)}) copy-start(f32[4,6]{1,0:T(4,128)} %param.23) | copy-start | bytes 292
  7.3 115.7 %copy-start.15 = (f32[4,6]{1,0:T(4,128)S(1)}, f32[4,6]{1,0:T(4,128)}, u32[]{:S(2)}) copy-start(f32[4,6]{1,0:T(4,128)} %param.31) | copy-start | bytes 292
  7.3 115.7 %copy-start.16 = (f32[4,6]{1,0:T(4,128)S(1)}, f32[4,6]{1,0:T(4,128)}, u32[]{:S(2)}) copy-start(f32[4,6]{1,0:T(4,128)} %param.27) | copy-start | bytes 292
  7.3 483.6 %copy-start.6 = (f32[64,384]{1,0:T(8,128)S(1)}, f32[64,384]{1,0:T(8,128)}, u32[]{:S(2)}) copy-start(f32[64,384]{1,0:T(8,128)} %param.28) | copy-start | bytes 294916
  7.3 483.6 %copy-start.7 = (f32[64,384]{1,0:T(8,128)S(1)}, f32[64,384]{1,0:T(8,128)}, u32[]{:S(2)}) copy-start(f32[64,384]{1,0:T(8,128)} %param.24) | copy-start | bytes 294916
  7.9 483.0 %copy-start = (f32[64,384]{1,0:T(8,128)S(1)}, f32[64,384]{1,0:T(8,128)}, u32[]{:S(2)}) copy-start(f32[64,384]{1,0:T(8,128)} %param.20) | copy-start | bytes 294916
  491.0 1.7 copy-start.1
  491.0 1.7 copy-start.8
  491.0 1.7 copy-start.9
  492.7 22.6 %copy-start.2 = (f32[64,384]{1,0:T(8,128)}, f32[64,384]{1,0:T(8,128)S(1)}, u32[]{:S(2)}) copy-start(f32[64,384]{1,0:T(8,128)S(1)} %get-tuple-element.100) | copy-start | bytes 294916
  492.7 22.6 %copy-start.3 = (f32[64,384]{1,0:T(8,128)}, f32[64,384]{1,0:T(8,128)S(1)}, u32[]{:S(2)}) copy-start(f32[64,384]{1,0:T(8,128)S(1)} %get-tuple-element.96) | copy-start | bytes 294916
  494.4 35.6 %copy-start.4 = (f32[48,512]{1,0:T(8,128)}, f32[48,512]{1,0:T(8,128)S(1)}, u32[]{:S(2)}) copy-start(f32[48,512]{1,0:T(8,128)S(1)} %get-tuple-element.101) | copy-start | bytes 294916
  494.4 35.6 %copy-start.5 = (f32[48,512]{1,0:T(8,128)}, f32[48,512]{1,0:T(8,128)S(1)}, u32[]{:S(2)}) copy-start(f32[48,512]{1,0:T(8,128)S(1)} %get-tuple-element.97) | copy-start | bytes 294916
  514.1 0.6 copy-start.10
Sparse Core Ops, SparseCore 0:
  13.4 477.5 all-reduce.5
where the time goes:
time: 581 us; the launch traced here: 580 us
  waiting for transfers between devices  367 us (63%)
  blocking collectives  174 us (30%)
  between operations  17.4 us (3%)
  other arithmetic  16.7 us (3%)
    psum x1, waiting for transfers between devices, on_device(): lax.psum((gradients[0], gradients[1], gradients[2], gradients[3]), ('repl...  367 us
    psum x1, blocking collectives, on_device(): lax.psum((gradients[0], gradients[1], gradients[2], gradients[3]), ('repl...  112 us
    psum x1, blocking collectives, on_device(): lax.psum((weight_squares[member], update_squares[member]), 'shard')  14.6 us
    all_gather x1, blocking collectives, on_device(): lax.all_gather(shards[0], 'shard', axis=0, tiled=True)  14 us
    all_gather x1, blocking collectives, on_device(): lax.all_gather(shards[1], 'shard', axis=0, tiled=True)  13 us
    unnamed x1, blocking collectives  12.5 us
  transfers between devices with their start and end apart: 1, of which 1 were waited for; matrix products, arithmetic and copies ran while one was open for 1% of the time, Pallas kernels for 0%

commit v1 on v0

--- a/solution.py
+++ b/solution.py
@@ -35,7 +35,7 @@
     decay_rates = (0.01, 0.01, 0.0, 0.0)
     gradients = (grad_query[0], grad_output[0], grad_norm[0], grad_bias[0])
     totals = lax.psum(
-        (gradients[0], gradients[1], gradients[2], gradients[3]), ("replica", "shard")
+        lax.psum((gradients[0], gradients[1], gradients[2], gradients[3]), "replica"), "shard"
     )
     position = lax.axis_index("shard")
     summed_all = tuple(

time: 581 us -> 688 us (1.18)
  blocking collectives: 174 us -> 370 us
  waiting for transfers between devices: 367 us -> 277 us
    psum x1 -> x2, blocking collectives: 112 us -> 307 us  [the longest x1 222 us: on_device(): lax.psum((gradients[0], gradients[1], gradients[2], gradients[3]), 'repli...]
    psum x1 -> x2, waiting for transfers between devices: 367 us -> 276 us  [the longest x1 276 us: on_device(): lax.psum((gradients[0], gradients[1], gradients[2], gradients[3]), 'repli...]
  transfers between devices with their start and end apart: 1 -> 2, of which waited for: 1 -> 1; matrix products, arithmetic and copies ran while one was open for 1% -> 1% of each run, Pallas kernels for 0% -> 0%
where the time goes in v1:
time: 688 us; the launch traced here: 687 us
  blocking collectives  370 us (54%)
  waiting for transfers between devices  277 us (40%)
  between operations  17.4 us (3%)
  other arithmetic  16.7 us (2%)
    psum x1, waiting for transfers between devices, on_device(): lax.psum((gradients[0], gradients[1], gradients[2], gradients[3]), 'repli...  276 us
    psum x1, blocking collectives, on_device(): lax.psum((gradients[0], gradients[1], gradients[2], gradients[3]), 'repli...  222 us
    psum x1, blocking collectives, on_device(): lax.psum(lax.psum((gradients[0], gradients[1], gradients[2], gradients[3]...  85.2 us
    psum x1, blocking collectives, on_device(): lax.psum((weight_squares[member], update_squares[member]), 'shard')  16 us
  transfers between devices with their start and end apart: 2, of which 1 were waited for; matrix products, arithmetic and copies ran while one was open for 1% of the time, Pallas kernels for 0%

profile of v1, /device:TPU:1, one launch (start us, length us, event | category | flops | bytes accessed | tf_op | source)
XLA Modules:
  0.0 687.5 jit_solution(7431582791191107202)
XLA Ops:
  7.2 0.0 all-reduce.9.cloned.1.call-start
  7.2 0.7 all-reduce.9.cloned.1.call-update
  7.9 0.0 all-reduce.11.cloned.1.call-start
  8.0 276.4 %all-reduce.9.cloned.1.call-done = (f32[384,512]{1,0:T(8,128)}, f32[512,384]{1,0:T(8,128)}) async-done(((f32[384,512]{1,0:T(8,128)}, f32[512,384]{1,0:T(8,128)}), (f32[384,512]{1,0:T(8,128)}, f32[512,384]{1,0:T(8,128)})) %all-reduce.9.cloned.1.call-update) | async-done | bytes 1572880 | tf_op jit(solution)/shard_map/psum | solution.py:38
  284.4 0.0 copy-start.12
  284.4 0.0 copy-start.13
  284.4 0.0 copy-start.17
  284.4 0.0 copy-start.18
  284.4 0.0 copy-start.6
  284.4 0.0 copy-start.7
  284.4 0.0 all-reduce.11.cloned.1.call-update
  284.4 0.0 copy-start
  284.4 0.6 copy-done.12
  285.1 0.1 copy.32
  285.1 1.3 dynamic-slice
  287.1 0.0 copy-done.13
  287.1 0.0 copy-start.11
  287.1 0.0 copy-start.15
  287.1 0.0 copy-start.16
  287.1 221.7 %all-reduce.1 = (f32[32,6]{1,0:T(8,128)S(1)}, f32[512]{0:T(512)S(1)}) all-reduce(f32[32,6]{1,0:T(8,128)S(1)} %bitcast.30, f32[512]{0:T(512)S(1)} %bitcast.32), channel_id=1, replica_groups=mesh['replica'=64,'shard'=8] {'replica'}, use_global_device_ids=true, to_apply=%region_20.0 | all-reduce | flops 704 | bytes 5632 | tf_op jit(solution)/shard_map/psum | solution.py:38
  508.8 85.2 %all-reduce.4 = (f32[32,6]{1,0:T(8,128)S(1)}, f32[512]{0:T(512)S(1)}) all-reduce(f32[32,6]{1,0:T(8,128)S(1)} %get-tuple-element.46, f32[512]{0:T(512)S(1)} %get-tuple-element.47), channel_id=1, replica_groups=mesh['replica'=64,'shard'=8] {'shard'}, use_global_device_ids=true, to_apply=%region_21.0 | all-reduce | flops 704 | bytes 5632 | tf_op jit(solution)/shard_map/psum | solution.py:37
  594.0 0.0 copy-start.14
  594.0 0.0 copy-done.17
  594.0 0.0 copy-done.18
  594.0 0.6 copy-done.14
  594.6 1.2 multiply_reduce_fusion.6
  595.8 0.0 copy-done.11
  595.8 0.0 copy-done.15
  595.8 0.0 copy-done.16
  595.8 1.2 multiply_reduce_fusion.4
  597.0 0.0 all-reduce.11.cloned.1.call-done
  597.0 0.0 copy-done.6
  597.0 0.0 copy-done.7
  597.0 0.0 copy-done
  597.0 0.0 copy-start.1
  597.1 0.0 copy-start.8
  597.1 0.0 copy-start.9
  597.1 1.7 multiply_reduce_fusion.1
  598.8 0.0 copy-start.2
  598.8 0.0 copy-done.1
  598.8 0.0 copy-done.8
  598.8 0.0 copy-done.9
  598.8 1.6 multiply_reduce_fusion
  600.5 16.0 %all-reduce.3 = (f32[]{:T(128)}, f32[]{:T(128)}, f32[]{:T(128)}, f32[]{:T(128)}, f32[]{:T(128)}, /*index=5*/f32[]{:T(128)}, f32[]{:T(128)}, f32[]{:T(128)}) all-reduce(f32[]{:T(128)} %get-tuple-element.74, f32[]{:T(128)} %get-tuple-element.79, f32[]{:T(128)} %get-tuple-element.45, ...), channel_id=1, replica_groups=mesh['replica'=64,'shard'=8] {'shard'}, use_global_device_ids=true, to_apply=%region_7.0 | all-reduce | flops 8 | bytes 64 | tf_op jit(solution)/shard_map/psum | solution.py:60
  616.5 5.1 fusion.5
  621.6 0.0 copy-start.10
  621.7 0.6 fusion.11
  622.3 0.0 copy-done.10
  622.8 0.0 copy-done.2
  622.8 0.0 copy-done.3
  622.8 0.1 subtract_convert_fusion.1
  622.9 13.5 %all_gather.12 = bf16[512,384]{1,0:T(8,128)(2,1)S(1)} all-gather(bf16[64,384]{1,0:T(8,128)(2,1)S(1)} %subtract_convert_fusion.1), channel_id=1, replica_groups=mesh['replica'=64,'shard'=8] {'shard'}, dimensions={0}, use_global_device_ids=true | all-gather | bytes 442368 | tf_op jit(solution)/shard_map/all_gather | solution.py:74
  637.0 0.0 copy-done.4
  637.0 0.0 copy-done.5
  637.0 0.1 subtract_convert_fusion
  637.1 13.0 %all_gather.13 = bf16[384,512]{1,0:T(8,128)(2,1)S(1)} all-gather(bf16[48,512]{1,0:T(8,128)(2,1)S(1)} %subtract_convert_fusion), channel_id=1, replica_groups=mesh['replica'=64,'shard'=8] {'shard'}, dimensions={0}, use_global_device_ids=true | all-gather | bytes 442368 | tf_op jit(solution)/shard_map/all_gather | solution.py:75
  650.7 0.2 dynamic-update-slice
  651.0 12.5 %all-reduce = bf16[512]{0:T(512)(128)(2,1)} all-reduce(bf16[512]{0:T(512)(128)(2,1)S(1)} %dynamic-update-slice), channel_id=1, replica_groups=mesh['replica'=64,'shard'=8] {'shard'}, use_global_device_ids=true, to_apply=%add | all-reduce | flops 512 | bytes 2048
  664.1 8.6 %all-gather = bf16[8,4,6]{2,1,0:T(4,128)(2,1)S(1)} all-gather(bf16[1,4,6]{2,1,0:T(4,128)(2,1)S(1)} %fusion.3), channel_id=1, replica_groups=mesh['replica'=64,'shard'=8] {'shard'}, dimensions={0}, use_global_device_ids=true | all-gather | bytes 432 | tf_op jit(solution)/shard_map/all_gather | solution.py:77
  672.8 0.7 copy.33
  673.4 5.1 maximum_sqrt_fusion.2
  678.6 0.6 pad_maximum_fusion
  679.1 0.7 copy.43
  679.9 0.7 copy.44
  (6 shorter events, 0.0 us)
Async XLA Ops:
  7.2 277.2 %all-reduce.9.cloned.1.call-start = ((), (), s32[]{:S(2)}) async-start(), calls=%async_computation | async-start | bytes 3145728 | tf_op jit(solution)/shard_map/psum | solution.py:38
  7.9 589.1 %all-reduce.11.cloned.1.call-start = ((), (), s32[]{:S(2)}) async-start(), calls=%async_computation.1 | async-start | bytes 3145728 | tf_op jit(solution)/shard_map/psum | solution.py:37
  284.4 0.7 copy-start.12
  284.4 2.7 copy-start.13
  284.4 309.6 %copy-start.17 = (f32[64]{0:T(128)S(1)}, f32[64]{0:T(128)}, u32[]{:S(2)}) copy-start(f32[64]{0:T(128)} %param.30) | copy-start | bytes 772
  284.4 309.6 %copy-start.18 = (f32[64]{0:T(128)S(1)}, f32[64]{0:T(128)}, u32[]{:S(2)}) copy-start(f32[64]{0:T(128)} %param.26) | copy-start | bytes 772
  284.4 312.7 %copy-start.6 = (f32[64,384]{1,0:T(8,128)S(1)}, f32[64,384]{1,0:T(8,128)}, u32[]{:S(2)}) copy-start(f32[64,384]{1,0:T(8,128)} %param.28) | copy-start | bytes 294916
  284.4 312.7 %copy-start.7 = (f32[64,384]{1,0:T(8,128)S(1)}, f32[64,384]{1,0:T(8,128)}, u32[]{:S(2)}) copy-start(f32[64,384]{1,0:T(8,128)} %param.24) | copy-start | bytes 294916
  284.4 312.6 %copy-start = (f32[64,384]{1,0:T(8,128)S(1)}, f32[64,384]{1,0:T(8,128)}, u32[]{:S(2)}) copy-start(f32[64,384]{1,0:T(8,128)} %param.20) | copy-start | bytes 294916
  287.1 308.8 %copy-start.11 = (f32[4,6]{1,0:T(4,128)S(1)}, f32[4,6]{1,0:T(4,128)}, u32[]{:S(2)}) copy-start(f32[4,6]{1,0:T(4,128)} %param.23) | copy-start | bytes 292
  287.1 308.8 %copy-start.15 = (f32[4,6]{1,0:T(4,128)S(1)}, f32[4,6]{1,0:T(4,128)}, u32[]{:S(2)}) copy-start(f32[4,6]{1,0:T(4,128)} %param.31) | copy-start | bytes 292
  287.1 308.8 %copy-start.16 = (f32[4,6]{1,0:T(4,128)S(1)}, f32[4,6]{1,0:T(4,128)}, u32[]{:S(2)}) copy-start(f32[4,6]{1,0:T(4,128)} %param.27) | copy-start | bytes 292
  594.0 0.7 copy-start.14
  597.0 1.8 copy-start.1
  597.1 1.8 copy-start.8
  597.1 1.7 copy-start.9
  598.8 24.0 %copy-start.2 = (f32[64,384]{1,0:T(8,128)}, f32[64,384]{1,0:T(8,128)S(1)}, u32[]{:S(2)}) copy-start(f32[64,384]{1,0:T(8,128)S(1)} %get-tuple-element.104) | copy-start | bytes 294916
  598.8 24.0 %copy-start.3 = (f32[64,384]{1,0:T(8,128)}, f32[64,384]{1,0:T(8,128)S(1)}, u32[]{:S(2)}) copy-start(f32[64,384]{1,0:T(8,128)S(1)} %get-tuple-element.100) | copy-start | bytes 294916
  600.5 36.5 %copy-start.4 = (f32[48,512]{1,0:T(8,128)}, f32[48,512]{1,0:T(8,128)S(1)}, u32[]{:S(2)}) copy-start(f32[48,512]{1,0:T(8,128)S(1)} %get-tuple-element.105) | copy-start | bytes 294916
  600.5 36.5 %copy-start.5 = (f32[48,512]{1,0:T(8,128)}, f32[48,512]{1,0:T(8,128)S(1)}, u32[]{:S(2)}) copy-start(f32[48,512]{1,0:T(8,128)S(1)} %get-tuple-element.101) | copy-start | bytes 294916
  621.6 0.6 copy-start.10
Sparse Core Ops, SparseCore 0:
  11.5 272.8 all-reduce.8
  286.8 82.2 all-reduce.10
